TPU v7x, 256 devices: a whole 4x4x8 slice. The times are simulated.
256 devices in a mesh: blk: 32 (over z, x_lo, core), col: 8 (over x_hi, y).
Axes of the slice: x: 4 (x_hi: 2, x_lo: 2; x = x_hi * 2 + x_lo), y: 4, z: 8, core: 2. Of those that a mesh axis runs over, the one named last changes fastest.
Arguments:
- feat1: bfloat16 [128, 384, 256], P('blk', 'col'), may hold values from -40 to 40
- feat2: bfloat16 [128, 384, 256], P('blk', 'col'), may hold values from -40 to 40
Outputs:
- flow: float32 [2, 128, 384], P(None, 'blk', 'col')
- grad_flow: float32 [2, 128, 384], P(None, 'blk', 'col')
- grad_warped: float32 [128, 384, 256], P('blk', 'col')
All inputs are finite; a program needn't handle non-finite values.
Results may differ from a plain program's by a relative error of at most 0.0075.
Values may be sent and summed in bfloat16 or wider, within the bound.
No kernel may reach another device: no remote copies, remote signals or barrier semaphores. Data moves between devices by JAX's collectives and lax.ppermute only.
A program may use at most 64 MiB of HBM per device.

v0:
```python
import math
import jax
import jax.numpy as jnp
from jax import lax
from jax.sharding import PartitionSpec as P

ssim_one = 0.01
ssim_two = 0.03
charb_sq = 0.0001


def with_halo(value, sides, width):
    for axis, dim in sides:
        count, length = (lax.axis_size(axis), value.shape[dim])
        up = [(i, (i + 1) % count) for i in range(count - 1)]
        down = [(j, i) for i, j in up]
        last = lax.slice_in_dim(value, length - width, length, axis=dim)
        first = lax.slice_in_dim(value, 0, width, axis=dim)
        before = lax.ppermute(last, axis, up)
        after = lax.ppermute(first, axis, down)
        value = jnp.concatenate([before, value, after], axis=dim)
    return value


def box_valid(padded):
    rows_out = padded.shape[0] - 2
    cols_out = padded.shape[1] - 2
    total = jnp.zeros((rows_out, cols_out) + padded.shape[2:], padded.dtype)
    for offset_r in range(3):
        for offset_c in range(3):
            total = total + padded[offset_r : offset_r + rows_out, offset_c : offset_c + cols_out]
    return total / 9.0


def ssim_loss(mean_y, var_y, cov_xy, mean_x, var_x):
    top = (2.0 * mean_x * mean_y + ssim_one) * (2.0 * cov_xy + ssim_two)
    bottom = (mean_x * mean_x + mean_y * mean_y + ssim_one) * (var_x + var_y + ssim_two)
    return jnp.sum((1.0 - top / bottom) * 0.5)


def local_terms(xpad, ypad):
    mean_x = box_valid(xpad)
    mean_y = box_valid(ypad)
    var_x = box_valid(xpad * xpad) - mean_x * mean_x
    var_y = box_valid(ypad * ypad) - mean_y * mean_y
    cov_xy = box_valid(xpad * ypad) - mean_x * mean_y
    loss, pull = jax.vjp(
        lambda one, two, three: ssim_loss(one, two, three, mean_x, var_x), mean_y, var_y, cov_xy
    )
    grad_mean, grad_var, grad_cov = pull(jnp.ones_like(loss))
    first = grad_mean - 2.0 * grad_var * mean_y - grad_cov * mean_x
    return (first, grad_var, grad_cov)


def edge_weight(lower, upper):
    return jnp.exp(-jnp.mean(jnp.abs(upper - lower), axis=-1))


def charbonnier(weight, delta):
    return weight * delta / jnp.sqrt(delta * delta + charb_sq)


def absorb(carry, queries, keys, key_y, key_x, scale):
    total_keys = keys.shape[0]
    width = keys.shape[1]
    step = min(total_keys, 2048)
    while total_keys % step != 0:
        step = step - 1
    blocks = total_keys // step

    def visit(state, item):
        top, total, acc, along_y, along_x = state
        key_block, block_y, block_x = item
        score = (
            lax.dot_general(
                queries, key_block, (((1,), (1,)), ((), ())), preferred_element_type=jnp.float32
            )
            * scale
        )
        new_top = jnp.maximum(top, jnp.max(score, axis=1))
        shrink = jnp.exp(top - new_top)
        expo = jnp.exp(score - new_top[:, None])
        total = total * shrink + jnp.sum(expo, axis=1)
        acc = acc * shrink[:, None] + jnp.dot(
            expo.astype(jnp.bfloat16), key_block, preferred_element_type=jnp.float32
        )
        along_y = along_y * shrink + jnp.sum(expo * block_y[None, :], axis=1)
        along_x = along_x * shrink + jnp.sum(expo * block_x[None, :], axis=1)
        return ((new_top, total, acc, along_y, along_x), None)

    items = (
        keys.reshape(blocks, step, width),
        key_y.reshape(blocks, step),
        key_x.reshape(blocks, step),
    )
    carry, unused = lax.scan(visit, carry, items)
    return carry


def body(feat1, feat2):
    rows, cols, width = feat1.shape
    ncol = lax.axis_size("col")
    full_rows = rows * lax.axis_size("blk")
    full_cols = cols * ncol
    row_start = lax.axis_index("blk") * rows
    col_start = lax.axis_index("col") * cols
    scale = 1.0 / math.sqrt(width)
    tokens = rows * cols
    queries = feat1.reshape(tokens, width)
    init = (
        jnp.full((tokens,), -1e30, jnp.float32),
        jnp.zeros((tokens,), jnp.float32),
        jnp.zeros((tokens, width), jnp.float32),
        jnp.zeros((tokens,), jnp.float32),
        jnp.zeros((tokens,), jnp.float32),
    )

    def norm_y(index):
        return (index.astype(jnp.float32) + 0.5) * (2.0 / full_rows) - 1.0

    def norm_x(index):
        return (index.astype(jnp.float32) + 0.5) * (2.0 / full_cols) - 1.0

    piece = lax.all_gather(feat2, ("blk", "col"), axis=0, tiled=True)
    count = piece.shape[0]
    gathered = jnp.arange(count, dtype=jnp.int32)
    shard = gathered // rows
    tile_y = shard // ncol * rows + gathered % rows
    tile_x = shard % ncol * cols
    grid_y = jnp.broadcast_to(tile_y[:, None], (count, cols))
    grid_x = tile_x[:, None] + jnp.arange(cols, dtype=jnp.int32)[None, :]
    carry = absorb(
        init,
        queries,
        piece.reshape(count * cols, width),
        norm_y(grid_y).reshape(-1),
        norm_x(grid_x).reshape(-1),
        scale,
    )
    top, total, acc, along_y, along_x = carry
    warped = (acc / total[:, None]).astype(jnp.bfloat16).reshape(rows, cols, width)
    own_y = norm_y(row_start + jnp.arange(rows, dtype=jnp.int32))
    own_x = norm_x(col_start + jnp.arange(cols, dtype=jnp.int32))
    flow = jnp.stack(
        [
            (along_y / total).reshape(rows, cols) - own_y[:, None],
            (along_x / total).reshape(rows, cols) - own_x[None, :],
        ]
    )
    pair = jnp.stack([feat1, warped])
    xval = feat1.astype(jnp.float32)
    yval = warped.astype(jnp.float32)
    margin = 1
    padded = with_halo(pair, (("blk", 1), ("col", 2)), 1)
    xpad = padded[0].astype(jnp.float32)
    ypad = padded[1].astype(jnp.float32)
    first, grad_var, grad_cov = local_terms(xpad, ypad)
    maps = jnp.stack([first, grad_var, grad_cov])
    beside_all = with_halo(maps.astype(jnp.bfloat16), (("blk", 1), ("col", 2)), 1).astype(
        maps.dtype
    )
    spread_first = box_valid(beside_all[0])
    spread_var = box_valid(beside_all[1])
    spread_cov = box_valid(beside_all[2])
    grad_warped = spread_first + 2.0 * yval * spread_var + xval * spread_cov
    flow_pad = with_halo(flow, (("blk", 1), ("col", 2)), 1)
    x_rows = xpad[margin - 1 : margin + rows + 1, margin : margin + cols]
    x_cols = xpad[margin : margin + rows, margin - 1 : margin + cols + 1]
    edge_y = row_start - 1 + jnp.arange(rows + 1, dtype=jnp.int32)
    valid_y = (edge_y >= 0) & (edge_y <= full_rows - 2)
    edge_x = col_start - 1 + jnp.arange(cols + 1, dtype=jnp.int32)
    valid_x = (edge_x >= 0) & (edge_x <= full_cols - 2)
    delta_y = flow_pad[:, 1:, 1:-1] - flow_pad[:, :-1, 1:-1]
    push_y = jnp.where(
        valid_y[None, :, None],
        charbonnier(edge_weight(x_rows[:-1], x_rows[1:])[None], delta_y),
        0.0,
    )
    delta_x = flow_pad[:, 1:-1, 1:] - flow_pad[:, 1:-1, :-1]
    push_x = jnp.where(
        valid_x[None, None, :],
        charbonnier(edge_weight(x_cols[:, :-1], x_cols[:, 1:])[None], delta_x),
        0.0,
    )
    grad_flow = push_y[:, :rows] - push_y[:, 1:] + push_x[:, :, :cols] - push_x[:, :, 1:]
    return (flow, grad_flow, grad_warped)


def solution(mesh):
    placed = (P("blk", "col", None), P("blk", "col", None))
    return jax.shard_map(
        body,
        mesh=mesh,
        in_specs=placed,
        out_specs=(P(None, "blk", "col"), P(None, "blk", "col"), P("blk", "col", None)),
        check_vma=False,
    )
```

profile of v0, /device:TPU:132, one launch (start us, length us, event | category | flops | bytes accessed | tf_op | source)
XLA Modules:
  0.0 919.5 jit_solution(4387927049897352818)
XLA Ops:
  9.2 743.5 %all-gather.2.cloned.1.call-done = bf16[1024,48,256]{2,1,0:T(8,128)(2,1)} async-done(((bf16[4,48,256]{2,1,0:T(8,128)(2,1)}), bf16[1024,48,256]{2,1,0:T(8,128)(2,1)}) %all-gather.2.cloned.1.call-update) | async-done | bytes 25165840 | tf_op jit(solution)/shard_map/all_gather | solution.py:124
  752.7 100.4 %while.19 = (s32[]{:T(128)}, f32[192]{0:T(256)S(1)}, f32[192]{0:T(256)S(1)}, f32[192,256]{1,0:T(8,128)S(1)}, f32[192]{0:T(256)S(1)}, /*index=5*/f32[192]{0:T(256...) while((s32[]{:T(128)}, f32[192]{0:T(256)S(1)}, ...), condition=%wide.region_5.6_spmd.clone, body=%wide.region_0.5_spmd.clone.sunk | while | flops 406734528 | bytes 7375766 | solution.py:96
  756.9 1.8 fusion.87
  769.5 1.8 fusion.87
  777.9 1.8 fusion.87
  786.2 1.8 fusion.87
  794.6 1.8 fusion.87
  803.0 1.8 fusion.87
  811.3 1.8 fusion.87
  853.4 4.2 collective-permute-start.4
  857.6 1.9 collective-permute-start.5
  860.3 5.7 collective-permute-start.1
  866.0 1.9 collective-permute-start
  868.0 5.5 collective-permute-done
  873.5 1.9 collective-permute-start.3
  875.5 3.9 collective-permute-start.2
  879.5 1.9 collective-permute-start.7
  881.4 7.5 collective-permute-start.6
  890.5 1.9 collective-permute-start.9
  892.4 2.4 collective-permute-start.8
  895.0 5.2 collective-permute-done.8
  900.2 1.9 collective-permute-start.11
  902.1 3.9 collective-permute-start.10
  906.7 4.7 collective-permute-done.10
  (241 shorter events, 92.9 us)
Async XLA Ops:
  7.2 745.6 %copy-start = (bf16[4,48,256]{2,1,0:T(8,128)(2,1)S(1)}, bf16[4,48,256]{2,1,0:T(8,128)(2,1)}, u32[]{:S(2)}) copy-start(bf16[4,48,256]{2,1,0:T(8,128)(2,1)} %param.4) | copy-start | bytes 294916
  7.2 745.6 %all-gather.2.cloned.1.call-start = ((), (), s32[]{:S(2)}) async-start(), calls=%async_computation | async-start | bytes 25264128 | tf_op jit(solution)/shard_map/all_gather | solution.py:124
  853.4 14.5 %collective-permute-start.4 = (f32[2,1,48]{2,1,0:T(1,128)S(1)}, f32[2,1,48]{2,1,0:T(1,128)S(1)}, u32[]{:S(2)}, u32[]{:S(2)}) collective-permute-start(f32[2,1,48]{2,1,0:T(1,128)S(1)} %get-tuple-element.154), channel_id=1, source_target_pairs={{8,0},{16,8},{24,16},{32,24},{40,32},{48,40},{56,48},{64,56},{72,6... | collective-permute-start | bytes 1160 | tf_op jit(solution)/shard_map/ppermute | solution.py:20
  857.6 10.3 %collective-permute-start.5 = (f32[2,1,48]{2,1,0:T(1,128)S(1)}, f32[2,1,48]{2,1,0:T(1,128)S(1)}, u32[]{:S(2)}, u32[]{:S(2)}) collective-permute-start(f32[2,1,48]{2,1,0:T(1,128)S(1)} %get-tuple-element.153), channel_id=1, source_target_pairs={{0,8},{8,16},{16,24},{24,32},{32,40},{40,48},{48,56},{56,64},{64,7... | collective-permute-start | bytes 1160 | tf_op jit(solution)/shard_map/ppermute | solution.py:19
  860.3 7.7 collective-permute-start.1
  866.0 7.5 collective-permute-start
  873.5 15.4 %collective-permute-start.3 = (bf16[2,6,1,256]{3,2,1,0:T(2,128)(2,1)S(1)}, bf16[2,6,1,256]{3,2,1,0:T(2,128)(2,1)S(1)}, u32[]{:S(2)}, u32[]{:S(2)}) collective-permute-start(bf16[2,6,1,256]{3,2,1,0:T(2,128)(2,1)S(1)} %get-tuple-element.148), channel_id=1, source_target_pairs={{1,0},{2,1},{3,2},{4,3},{5,4},{6,5},{7,6},{9,8},{10,9},{11,10},{12... | collective-permute-start | bytes 18440 | tf_op jit(solution)/shard_map/ppermute | solution.py:20
  875.5 13.5 %collective-permute-start.2 = (bf16[2,6,1,256]{3,2,1,0:T(2,128)(2,1)S(1)}, bf16[2,6,1,256]{3,2,1,0:T(2,128)(2,1)S(1)}, u32[]{:S(2)}, u32[]{:S(2)}) collective-permute-start(bf16[2,6,1,256]{3,2,1,0:T(2,128)(2,1)S(1)} %get-tuple-element.147), channel_id=1, source_target_pairs={{0,1},{1,2},{2,3},{3,4},{4,5},{5,6},{6,7},{8,9},{9,10},{10,11},{11... | collective-permute-start | bytes 18440 | tf_op jit(solution)/shard_map/ppermute | solution.py:19
  879.5 15.4 %collective-permute-start.7 = (f32[2,6,1]{2,1,0:T(8,128)S(1)}, f32[2,6,1]{2,1,0:T(8,128)S(1)}, u32[]{:S(2)}, u32[]{:S(2)}) collective-permute-start(f32[2,6,1]{2,1,0:T(8,128)S(1)} %get-tuple-element.152), channel_id=1, source_target_pairs={{0,1},{1,2},{2,3},{3,4},{4,5},{5,6},{6,7},{8,9},{9,10},{10,11},{11... | collective-permute-start | bytes 152 | tf_op jit(solution)/shard_map/ppermute | solution.py:19
  881.4 13.5 %collective-permute-start.6 = (f32[2,6,1]{2,1,0:T(8,128)S(1)}, f32[2,6,1]{2,1,0:T(8,128)S(1)}, u32[]{:S(2)}, u32[]{:S(2)}) collective-permute-start(f32[2,6,1]{2,1,0:T(8,128)S(1)} %get-tuple-element.151), channel_id=1, source_target_pairs={{1,0},{2,1},{3,2},{4,3},{5,4},{6,5},{7,6},{9,8},{10,9},{11,10},{12... | collective-permute-start | bytes 152 | tf_op jit(solution)/shard_map/ppermute | solution.py:20
  890.5 4.5 collective-permute-start.9
  892.4 7.8 collective-permute-start.8
  900.2 6.5 collective-permute-start.11
  902.1 9.3 %collective-permute-start.10 = (bf16[3,6,1,256]{3,2,1,0:T(2,128)(2,1)S(1)}, bf16[3,6,1,256]{3,2,1,0:T(2,128)(2,1)S(1)}, u32[]{:S(2)}, u32[]{:S(2)}) collective-permute-start(bf16[3,6,1,256]{3,2,1,0:T(2,128)(2,1)S(1)} %get-tuple-element.138), channel_id=1, source_target_pairs={{0,1},{1,2},{2,3},{3,4},{4,5},{5,6},{6,7},{8,9},{9,10},{10,11},{11... | collective-permute-start | bytes 27656 | tf_op jit(solution)/shard_map/ppermute | solution.py:19
Sparse Core Ops, SparseCore 0:
  9.9 742.8 all-gather.1
where the time goes:
time: 922 us; the launch traced here: 919 us
  waiting for transfers between devices  760 us (82%)
  matrix products  83.4 us (9%)
  starting transfers between devices  39.2 us (4%)
  other arithmetic  19.7 us (2%)
  between operations  14.4 us (2%)
    all_gather x1, waiting for transfers between devices, body(): piece = lax.all_gather(feat2, ('blk', 'col'), axis=0, tiled=True)  744 us
    dot_general x24, matrix products, visit(): lax.dot_general(queries, key_block, (((1,), (1,)), ((), ())), preferred_e...  43.6 us
    dot_general x24, matrix products, visit(): jnp.dot(expo.astype(jnp.bfloat16), key_block, preferred_element_type=jnp....  39.8 us
    ppermute x6, starting transfers between devices, with_halo(): after = lax.ppermute(first, axis, down)  23.2 us
  transfers between devices with their start and end apart: 13, of which 4 were waited for; matrix products, arithmetic and copies ran while one was open for 0% of the time, Pallas kernels for 0%

commit v1 on v0

--- a/solution.py
+++ b/solution.py
@@ -3,6 +3,7 @@
 import jax.numpy as jnp
 from jax import lax
 from jax.sharding import PartitionSpec as P
+from jax.lax import all_to_all, psum
 
 ssim_one = 0.01
 ssim_two = 0.03
@@ -121,7 +122,13 @@
     def norm_x(index):
         return (index.astype(jnp.float32) + 0.5) * (2.0 / full_cols) - 1.0
 
-    piece = lax.all_gather(feat2, ("blk", "col"), axis=0, tiled=True)
+    samples = []
+    for _ in range(psum(1, axis_name=("blk", "col"))):
+        samples.append(feat2)
+    wide_out = all_to_all(
+        jnp.stack(samples, 0), axis_name=("blk", "col"), split_axis=0, concat_axis=0
+    )
+    piece = jnp.concatenate(wide_out, 0)
     count = piece.shape[0]
     gathered = jnp.arange(count, dtype=jnp.int32)
     shard = gathered // rows

time: 922 us -> 731 us (0.79)
  waiting for transfers between devices: 760 us -> 544 us
  starting transfers between devices: 39.2 us -> 63.9 us
  between operations: 14.4 us -> 1 us
  local copies, waits for them, and re-layouts: 1.86 us -> 11.1 us
    all_gather x1 -> x0, waiting for transfers between devices: 744 us -> none  [body(): piece = lax.all_gather(feat2, ('blk', 'col'), axis=0, tiled=True)]
    all_to_all x0 -> x1, waiting for transfers between devices: none -> 539 us  [body(): all_to_all(jnp.stack(samples, 0), axis_name=('blk', 'col'), split_axis=0,...]
    ppermute x6, waiting for transfers between devices: 15.4 us -> 0.02 us  [with_halo(): before = lax.ppermute(last, axis, up)]
    all_to_all x0 -> x1, starting transfers between devices: none -> 14.7 us  [body(): all_to_all(jnp.stack(samples, 0), axis_name=('blk', 'col'), split_axis=0,...]
    ppermute x6, starting transfers between devices: 23.2 us -> 35.8 us  [with_halo(): after = lax.ppermute(first, axis, down)]
    another operation x0 -> x1, local copies, waits for them, and re-layouts: none -> 9.26 us  [body(): jnp.stack(samples, 0)]
  transfers between devices with their start and end apart: 13 -> 13, of which waited for: 4 -> 4; matrix products, arithmetic and copies ran while one was open for 0% -> 1% of each run, Pallas kernels for 0% -> 0%
where the time goes in v1:
time: 731 us; the launch traced here: 724 us
  waiting for transfers between devices  544 us (74%)
  matrix products  83.6 us (11%)
  starting transfers between devices  63.9 us (9%)
  other arithmetic  19.6 us (3%)
  local copies, waits for them, and re-layouts  11.1 us (2%)
    all_to_all x1, waiting for transfers between devices, body(): all_to_all(jnp.stack(samples, 0), axis_name=('blk', 'col'), split_axis=0,...  539 us
    dot_general x24, matrix products, visit(): lax.dot_general(queries, key_block, (((1,), (1,)), ((), ())), preferred_e...  43.8 us
    dot_general x24, matrix products, visit(): jnp.dot(expo.astype(jnp.bfloat16), key_block, preferred_element_type=jnp....  39.8 us
    ppermute x6, starting transfers between devices, with_halo(): after = lax.ppermute(first, axis, down)  35.8 us
    all_to_all x1, starting transfers between devices, body(): all_to_all(jnp.stack(samples, 0), axis_name=('blk', 'col'), split_axis=0,...  14.7 us
  transfers between devices with their start and end apart: 13, of which 4 were waited for; matrix products, arithmetic and copies ran while one was open for 1% of the time, Pallas kernels for 0%

profile of v1, /device:TPU:132, one launch (start us, length us, event | category | flops | bytes accessed | tf_op | source)
XLA Modules:
  0.0 724.3 jit_solution(18203653512807761041)
XLA Ops:
  0.6 9.3 %stack.20 = bf16[256,4,48,256]{3,2,1,0:T(8,128)(2,1)} broadcast(bf16[4,48,256]{2,1,0:T(8,128)(2,1)} %param.5), dimensions={1,2,3} | broadcast | bytes 25264128 | tf_op jit(solution)/shard_map/stack | solution.py:129
  9.9 14.7 %all-to-all-start = ((bf16[256,4,48,256]{3,2,1,0:T(8,128)(2,1)}), bf16[256,4,48,256]{3,2,1,0:T(8,128)(2,1)}, u32[]{:S(2)}, u32[]{:S(2)}) async-start(bf16[256,4,48,256]{3,2,1,0:T(8,128)(2,1)} %stack.20), calls=%async_computation | async-start | bytes 50331648 | tf_op jit(solution)/shard_map/all_to_all | solution.py:128
  25.9 539.4 %all-to-all-done = bf16[256,4,48,256]{3,2,1,0:T(8,128)(2,1)} async-done(((bf16[256,4,48,256]{3,2,1,0:T(8,128)(2,1)}), bf16[256,4,48,256]{3,2,1,0:T(8,128)(2,1)}, u32[]{:S(2)}, u32[]{:S(2)}) %all-to-all-start) | async-done | bytes 25165856 | tf_op jit(solution)/shard_map/all_to_all | solution.py:128
  565.3 100.6 %while.19 = (s32[]{:T(128)}, f32[192]{0:T(256)S(1)}, f32[192]{0:T(256)S(1)}, f32[192,256]{1,0:T(8,128)S(1)}, f32[192]{0:T(256)S(1)}, /*index=5*/f32[192]{0:T(256...) while((s32[]{:T(128)}, f32[192]{0:T(256)S(1)}, ...), condition=%wide.region_5.6_spmd.clone, body=%wide.region_0.5_spmd.clone.sunk | while | flops 406734528 | bytes 7376774 | solution.py:97
  569.5 1.8 fusion.87
  573.7 1.8 fusion.87
  577.9 1.8 fusion.87
  582.1 1.8 fusion.87
  586.3 1.8 fusion.87
  594.7 1.8 fusion.87
  598.8 1.8 fusion.87
  603.0 1.8 fusion.87
  666.3 7.3 %collective-permute-start.4 = (f32[2,1,48]{2,1,0:T(1,128)S(1)}, f32[2,1,48]{2,1,0:T(1,128)S(1)}, u32[]{:S(2)}, u32[]{:S(2)}) collective-permute-start(f32[2,1,48]{2,1,0:T(1,128)S(1)} %get-tuple-element.154), channel_id=1, source_target_pairs={{8,0},{16,8},{24,16},{32,24},{40,32},{48,40},{56,48},{64,56},{72,6... | collective-permute-start | bytes 1160 | tf_op jit(solution)/shard_map/ppermute | solution.py:21
  673.6 1.9 collective-permute-start.5
  676.1 1.9 collective-permute-start
  678.1 5.8 collective-permute-start.1
  685.6 1.9 collective-permute-start.2
  687.5 7.5 %collective-permute-start.3 = (bf16[2,6,1,256]{3,2,1,0:T(2,128)(2,1)S(1)}, bf16[2,6,1,256]{3,2,1,0:T(2,128)(2,1)S(1)}, u32[]{:S(2)}, u32[]{:S(2)}) collective-permute-start(bf16[2,6,1,256]{3,2,1,0:T(2,128)(2,1)S(1)} %get-tuple-element.148), channel_id=1, source_target_pairs={{1,0},{2,1},{3,2},{4,3},{5,4},{6,5},{7,6},{9,8},{10,9},{11,10},{12... | collective-permute-start | bytes 18440 | tf_op jit(solution)/shard_map/ppermute | solution.py:21
  695.1 1.9 collective-permute-start.6
  697.0 3.9 collective-permute-start.7
  702.5 1.9 collective-permute-start.8
  704.4 5.8 collective-permute-start.9
  712.1 1.9 collective-permute-start.10
  714.1 7.5 %collective-permute-start.11 = (bf16[3,6,1,256]{3,2,1,0:T(2,128)(2,1)S(1)}, bf16[3,6,1,256]{3,2,1,0:T(2,128)(2,1)S(1)}, u32[]{:S(2)}, u32[]{:S(2)}) collective-permute-start(bf16[3,6,1,256]{3,2,1,0:T(2,128)(2,1)S(1)} %get-tuple-element.139), channel_id=1, source_target_pairs={{1,0},{2,1},{3,2},{4,3},{5,4},{6,5},{7,6},{9,8},{10,9},{11,10},{12... | collective-permute-start | bytes 27656 | tf_op jit(solution)/shard_map/ppermute | solution.py:21
  (241 shorter events, 94.7 us)
Async XLA Ops:
  9.9 555.4 %all-to-all-start = ((bf16[256,4,48,256]{3,2,1,0:T(8,128)(2,1)}), bf16[256,4,48,256]{3,2,1,0:T(8,128)(2,1)}, u32[]{:S(2)}, u32[]{:S(2)}) async-start(bf16[256,4,48,256]{3,2,1,0:T(8,128)(2,1)} %stack.20), calls=%async_computation | async-start | bytes 50331648 | tf_op jit(solution)/shard_map/all_to_all | solution.py:128
  24.6 540.7 %copy-start = (bf16[4,48,256]{2,1,0:T(8,128)(2,1)S(1)}, bf16[4,48,256]{2,1,0:T(8,128)(2,1)}, u32[]{:S(2)}) copy-start(bf16[4,48,256]{2,1,0:T(8,128)(2,1)} %param.4) | copy-start | bytes 294916
  666.3 17.5 %collective-permute-start.4 = (f32[2,1,48]{2,1,0:T(1,128)S(1)}, f32[2,1,48]{2,1,0:T(1,128)S(1)}, u32[]{:S(2)}, u32[]{:S(2)}) collective-permute-start(f32[2,1,48]{2,1,0:T(1,128)S(1)} %get-tuple-element.154), channel_id=1, source_target_pairs={{8,0},{16,8},{24,16},{32,24},{40,32},{48,40},{56,48},{64,56},{72,6... | collective-permute-start | bytes 1160 | tf_op jit(solution)/shard_map/ppermute | solution.py:21
  673.6 10.2 %collective-permute-start.5 = (f32[2,1,48]{2,1,0:T(1,128)S(1)}, f32[2,1,48]{2,1,0:T(1,128)S(1)}, u32[]{:S(2)}, u32[]{:S(2)}) collective-permute-start(f32[2,1,48]{2,1,0:T(1,128)S(1)} %get-tuple-element.153), channel_id=1, source_target_pairs={{0,8},{8,16},{16,24},{24,32},{32,40},{40,48},{48,56},{56,64},{64,7... | collective-permute-start | bytes 1160 | tf_op jit(solution)/shard_map/ppermute | solution.py:20
  676.1 7.7 %collective-permute-start = (bf16[2,1,48,256]{3,2,1,0:T(8,128)(2,1)S(1)}, bf16[2,1,48,256]{3,2,1,0:T(8,128)(2,1)S(1)}, u32[]{:S(2)}, u32[]{:S(2)}) collective-permute-start(bf16[2,1,48,256]{3,2,1,0:T(8,128)(2,1)S(1)} %get-tuple-element.149), channel_id=1, source_target_pairs={{0,8},{8,16},{16,24},{24,32},{32,40},{40,48},{48,56},{56,64},{64,7... | collective-permute-start | bytes 147464 | tf_op jit(solution)/shard_map/ppermute | solution.py:20
  678.1 7.5 %collective-permute-start.1 = (bf16[2,1,48,256]{3,2,1,0:T(8,128)(2,1)S(1)}, bf16[2,1,48,256]{3,2,1,0:T(8,128)(2,1)S(1)}, u32[]{:S(2)}, u32[]{:S(2)}) collective-permute-start(bf16[2,1,48,256]{3,2,1,0:T(8,128)(2,1)S(1)} %get-tuple-element.150), channel_id=1, source_target_pairs={{8,0},{16,8},{24,16},{32,24},{40,32},{48,40},{56,48},{64,56},{72,6... | collective-permute-start | bytes 147464 | tf_op jit(solution)/shard_map/ppermute | solution.py:21
  685.6 15.4 %collective-permute-start.2 = (bf16[2,6,1,256]{3,2,1,0:T(2,128)(2,1)S(1)}, bf16[2,6,1,256]{3,2,1,0:T(2,128)(2,1)S(1)}, u32[]{:S(2)}, u32[]{:S(2)}) collective-permute-start(bf16[2,6,1,256]{3,2,1,0:T(2,128)(2,1)S(1)} %get-tuple-element.147), channel_id=1, source_target_pairs={{0,1},{1,2},{2,3},{3,4},{4,5},{5,6},{6,7},{8,9},{9,10},{10,11},{11... | collective-permute-start | bytes 18440 | tf_op jit(solution)/shard_map/ppermute | solution.py:20
  687.5 13.5 %collective-permute-start.3 = (bf16[2,6,1,256]{3,2,1,0:T(2,128)(2,1)S(1)}, bf16[2,6,1,256]{3,2,1,0:T(2,128)(2,1)S(1)}, u32[]{:S(2)}, u32[]{:S(2)}) collective-permute-start(bf16[2,6,1,256]{3,2,1,0:T(2,128)(2,1)S(1)} %get-tuple-element.148), channel_id=1, source_target_pairs={{1,0},{2,1},{3,2},{4,3},{5,4},{6,5},{7,6},{9,8},{10,9},{11,10},{12... | collective-permute-start | bytes 18440 | tf_op jit(solution)/shard_map/ppermute | solution.py:21
  695.1 15.1 %collective-permute-start.6 = (f32[2,6,1]{2,1,0:T(8,128)S(1)}, f32[2,6,1]{2,1,0:T(8,128)S(1)}, u32[]{:S(2)}, u32[]{:S(2)}) collective-permute-start(f32[2,6,1]{2,1,0:T(8,128)S(1)} %get-tuple-element.151), channel_id=1, source_target_pairs={{1,0},{2,1},{3,2},{4,3},{5,4},{6,5},{7,6},{9,8},{10,9},{11,10},{12... | collective-permute-start | bytes 152 | tf_op jit(solution)/shard_map/ppermute | solution.py:21
  697.0 13.2 %collective-permute-start.7 = (f32[2,6,1]{2,1,0:T(8,128)S(1)}, f32[2,6,1]{2,1,0:T(8,128)S(1)}, u32[]{:S(2)}, u32[]{:S(2)}) collective-permute-start(f32[2,6,1]{2,1,0:T(8,128)S(1)} %get-tuple-element.152), channel_id=1, source_target_pairs={{0,1},{1,2},{2,3},{3,4},{4,5},{5,6},{6,7},{8,9},{9,10},{10,11},{11... | collective-permute-start | bytes 152 | tf_op jit(solution)/shard_map/ppermute | solution.py:20
  702.5 7.9 %collective-permute-start.8 = (bf16[3,1,48,256]{3,2,1,0:T(8,128)(2,1)S(1)}, bf16[3,1,48,256]{3,2,1,0:T(8,128)(2,1)S(1)}, u32[]{:S(2)}, u32[]{:S(2)}) collective-permute-start(bf16[3,1,48,256]{3,2,1,0:T(8,128)(2,1)S(1)} %get-tuple-element.145), channel_id=1, source_target_pairs={{0,8},{8,16},{16,24},{24,32},{32,40},{40,48},{48,56},{56,64},{64,7... | collective-permute-start | bytes 221192 | tf_op jit(solution)/shard_map/ppermute | solution.py:20
  704.4 7.7 %collective-permute-start.9 = (bf16[3,1,48,256]{3,2,1,0:T(8,128)(2,1)S(1)}, bf16[3,1,48,256]{3,2,1,0:T(8,128)(2,1)S(1)}, u32[]{:S(2)}, u32[]{:S(2)}) collective-permute-start(bf16[3,1,48,256]{3,2,1,0:T(8,128)(2,1)S(1)} %get-tuple-element.146), channel_id=1, source_target_pairs={{8,0},{16,8},{24,16},{32,24},{40,32},{48,40},{56,48},{64,56},{72,6... | collective-permute-start | bytes 221192 | tf_op jit(solution)/shard_map/ppermute | solution.py:21
  712.1 10.1 %collective-permute-start.10 = (bf16[3,6,1,256]{3,2,1,0:T(2,128)(2,1)S(1)}, bf16[3,6,1,256]{3,2,1,0:T(2,128)(2,1)S(1)}, u32[]{:S(2)}, u32[]{:S(2)}) collective-permute-start(bf16[3,6,1,256]{3,2,1,0:T(2,128)(2,1)S(1)} %get-tuple-element.138), channel_id=1, source_target_pairs={{0,1},{1,2},{2,3},{3,4},{4,5},{5,6},{6,7},{8,9},{9,10},{10,11},{11... | collective-permute-start | bytes 27656 | tf_op jit(solution)/shard_map/ppermute | solution.py:20
  714.1 9.0 %collective-permute-start.11 = (bf16[3,6,1,256]{3,2,1,0:T(2,128)(2,1)S(1)}, bf16[3,6,1,256]{3,2,1,0:T(2,128)(2,1)S(1)}, u32[]{:S(2)}, u32[]{:S(2)}) collective-permute-start(bf16[3,6,1,256]{3,2,1,0:T(2,128)(2,1)S(1)} %get-tuple-element.139), channel_id=1, source_target_pairs={{1,0},{2,1},{3,2},{4,3},{5,4},{6,5},{7,6},{9,8},{10,9},{11,10},{12... | collective-permute-start | bytes 27656 | tf_op jit(solution)/shard_map/ppermute | solution.py:21
